TPU v7x, 512 devices: a whole 4x8x8 slice. The times are simulated.
512 devices in a mesh: tm: 32 (over x, y), space: 16 (over z, core).
Axes of the slice: x: 4, y: 8, z: 8, core: 2. Of those that a mesh axis runs over, the one named last changes fastest.
Arguments:
- data: bfloat16 [4096, 131072], P('tm', 'space'), may hold values from -40 to 40
- weights: float32 [131072], P('space'), may hold values from 1 to 30
- freqs: int32 [32], replicated, may hold values from 0 to 32, as said below
- n_keep: int32 [32], replicated, may hold values from 1 to 64, as said below
Outputs:
- mode_field: bfloat16 [32, 2, 64, 131072], P('tm', None, None, 'space')
- energy: float32 [32], P('tm')
Inputs may be any that keep to these rules, and one draw needn't show every extreme that they name: `freqs`: 32 distinct bins, among them 0 and 32, in an order drawn from the seed. `n_keep`: some frequency keeps all 64 columns and another keeps one.
All inputs are finite; a program needn't handle non-finite values.
Results may differ from a plain program's by a relative error of at most 0.0052.
Values may be sent and summed in bfloat16 or wider, within the bound.
No kernel may reach another device: no remote copies, remote signals or barrier semaphores. Data moves between devices by JAX's collectives and lax.ppermute only.
A program may use at most 64 MiB of HBM per device.

v0:
```python
import jax
import jax.numpy as jnp
from jax import lax
from jax.sharding import PartitionSpec as P

NT = 64
NS_STEPS = 4


def spectra_table(freqs):
    time_int = jnp.arange(NT, dtype=jnp.int32)
    time_float = time_int.astype(jnp.float32)
    window = 0.5 - 0.5 * jnp.cos(2.0 * jnp.pi * time_float / NT)
    norm = jnp.sqrt(jnp.sum(window * window))
    wrapped = freqs[:, None] * time_int[None, :] % NT
    phase_angle = 2.0 * jnp.pi * wrapped.astype(jnp.float32) / NT
    real_rows = window[None, :] * jnp.cos(phase_angle) / norm
    imag_rows = -window[None, :] * jnp.sin(phase_angle) / norm
    return jnp.concatenate([real_rows, imag_rows], axis=0).astype(jnp.bfloat16)


def transform_blocks(dft_table, snapshots, freq_count):
    block_count = snapshots.shape[0] // NT
    point_count = snapshots.shape[1]
    block_view = snapshots.reshape(block_count, NT, point_count)
    spectra = jnp.einsum("rt,btp->rbp", dft_table, block_view, preferred_element_type=jnp.float32)
    return spectra.reshape(2, freq_count, block_count, point_count)


def gram_terms(spectra, point_weights, total_points):
    spectra_re = spectra[0]
    spectra_im = spectra[1]
    stacked = jnp.concatenate([spectra_re, spectra_im], axis=1)
    square = (
        jnp.einsum(
            "fip,fjp->fij",
            stacked * point_weights[None, None, :],
            stacked,
            precision=lax.Precision.HIGHEST,
        )
        / total_points
    )
    return square


def unfold_terms(summed, block_count):
    g_one = summed[:, :block_count, :block_count] + summed[:, block_count:, block_count:]
    g_two = summed[:, :block_count, block_count:] - summed[:, block_count:, :block_count]
    return (g_one, g_two)


def inverse_root(embedded):
    size_two = embedded.shape[1]
    frobenius = jnp.sqrt(jnp.sum(embedded * embedded, axis=(1, 2)) + 1e-06)
    identity = jnp.broadcast_to(jnp.eye(size_two, dtype=jnp.float32), embedded.shape)
    current = embedded / frobenius[:, None, None]
    result = identity
    for sweep in range(NS_STEPS):
        factor = 1.5 * identity - 0.5 * jnp.einsum(
            "fij,fjk->fik", result, current, precision=lax.Precision.HIGHEST
        )
        current = jnp.einsum("fij,fjk->fik", current, factor, precision=lax.Precision.HIGHEST)
        result = jnp.einsum("fij,fjk->fik", factor, result, precision=lax.Precision.HIGHEST)
    return result


def finish_modes(spectra, summed, kept_counts, block_count):
    g_one, g_two = unfold_terms(summed, block_count)
    embedded = jnp.concatenate(
        [jnp.concatenate([g_one, -g_two], axis=2), jnp.concatenate([g_two, g_one], axis=2)], axis=1
    )
    inv_root = inverse_root(embedded)
    z_top = inv_root[:, :block_count, :block_count]
    z_low = inv_root[:, block_count:, :block_count]
    spectra_re = spectra[0]
    spectra_im = spectra[1]
    mode_re = jnp.einsum(
        "fij,fip->fjp", z_top, spectra_re, precision=lax.Precision.HIGHEST
    ) - jnp.einsum("fij,fip->fjp", z_low, spectra_im, precision=lax.Precision.HIGHEST)
    mode_im = jnp.einsum(
        "fij,fip->fjp", z_top, spectra_im, precision=lax.Precision.HIGHEST
    ) + jnp.einsum("fij,fip->fjp", z_low, spectra_re, precision=lax.Precision.HIGHEST)
    kept_mask = jnp.arange(block_count, dtype=jnp.int32)[None, :] < kept_counts[:, None]
    both_parts = jnp.stack([mode_re, mode_im], axis=1)
    mode_field = jnp.where(
        kept_mask[:, None, :, None], both_parts, jnp.zeros_like(both_parts)
    ).astype(jnp.bfloat16)
    energy = jnp.trace(g_one, axis1=1, axis2=2) / block_count
    return (mode_field, energy)


def shards(data, weights, freqs, n_keep):
    tm_count = lax.axis_size("tm")
    freq_count = freqs.shape[0]
    points_here = data.shape[1]
    total_points = points_here * lax.axis_size("space")
    block_count = data.shape[0] // NT * tm_count
    dft_table = spectra_table(freqs)
    spectra = transform_blocks(dft_table, data, freq_count)
    regrouped = lax.all_to_all(spectra, "tm", split_axis=1, concat_axis=2, tiled=True)
    partial_value = gram_terms(regrouped, weights, total_points)
    summed = lax.psum(partial_value, "space")
    kept_counts = lax.dynamic_slice_in_dim(n_keep, lax.axis_index("tm"), 1)
    mode_field, energy = finish_modes(regrouped, summed, kept_counts, block_count)
    return (mode_field, energy)


def solution(mesh):
    placed = (P("tm", "space"), P("space"), P(), P())
    return jax.shard_map(
        shards,
        mesh=mesh,
        in_specs=placed,
        out_specs=(P("tm", None, None, "space"), P("tm")),
        check_vma=False,
    )
```

profile of v0, /device:TPU:1, one launch (start us, length us, event | category | flops | bytes accessed | tf_op | source)
XLA Modules:
  0.0 300.4 jit_solution(1019790081844584022)
XLA Ops:
  7.2 0.7 multiply_reduce_fusion
  8.6 0.8 divide_convert_fusion.1
  9.4 0.7 fusion.36
  10.1 5.2 %copy.10 = f32[2,32,2,8192]{3,2,0,1:T(2,128)} copy(f32[2,32,2,8192]{3,1,2,0:T(8,128)S(1)} %fusion.36) | data formatting | bytes 8388608 | tf_op jit(solution)/shard_map/rt,btp->rbp/dot_general | solution.py:26
  15.3 10.7 %all-to-all-start = ((f32[2,32,2,8192]{3,2,0,1:T(2,128)}), f32[2,32,2,8192]{3,2,0,1:T(2,128)}, u32[]{:S(2)}, u32[]{:S(2)}) async-start(f32[2,32,2,8192]{3,2,0,1:T(2,128)} %copy.10), calls=%async_computation | async-start | bytes 8388608 | tf_op jit(solution)/shard_map/all_to_all | solution.py:100
  26.1 0.6 dynamic_slice.3
  26.7 92.0 %all-to-all-done = f32[2,32,2,8192]{3,2,0,1:T(2,128)} async-done(((f32[2,32,2,8192]{3,2,0,1:T(2,128)}), f32[2,32,2,8192]{3,2,0,1:T(2,128)}, u32[]{:S(2)}, u32[]{:S(2)}) %all-to-all-start) | async-done | bytes 4194336 | tf_op jit(solution)/shard_map/all_to_all | solution.py:100
  118.7 4.8 %fusion.35 = (f32[1,32,2,8192]{3,2,0,1:T(2,128)}, f32[1,32,2,8192]{3,2,0,1:T(2,128)}) fusion(f32[2,32,2,8192]{3,2,0,1:T(2,128)} %all-to-all-done), kind=kLoop, calls=%fused_computation.61 | loop fusion | bytes 8388608 | tf_op jit(solution)/shard_map/slice | solution.py:31
  123.5 5.2 %squeeze.8 = f32[1,64,8192]{2,0,1:T(1,128)} reshape(f32[1,32,2,8192]{3,2,0,1:T(2,128)} %get-tuple-element.6) | data formatting | bytes 4194304 | tf_op jit(solution)/shard_map/squeeze | solution.py:31
  128.7 3.7 %concatenate.53 = f32[64,8192]{1,0:T(8,128)} reshape(f32[1,32,2,8192]{3,2,0,1:T(2,128)} %get-tuple-element.6) | data formatting | bytes 4194304 | tf_op jit(solution)/shard_map/concatenate | solution.py:33
  132.4 5.2 %squeeze.9 = f32[1,64,8192]{2,0,1:T(1,128)} reshape(f32[1,32,2,8192]{3,2,0,1:T(2,128)} %get-tuple-element.7) | data formatting | bytes 4194304 | tf_op jit(solution)/shard_map/squeeze | solution.py:32
  137.6 3.6 %concatenate.54 = f32[64,8192]{1,0:T(8,128)} reshape(f32[1,32,2,8192]{3,2,0,1:T(2,128)} %get-tuple-element.7) | data formatting | bytes 4194304 | tf_op jit(solution)/shard_map/concatenate | solution.py:33
  141.3 12.4 %pad_maximum_fusion = f32[1,128,8192]{2,0,1:T(1,128)} fusion(f32[1,64,8192]{2,0,1:T(1,128)} %squeeze.9, f32[1,64,8192]{2,0,1:T(1,128)} %squeeze.8), kind=kLoop, calls=%fused_computation.8 | loop fusion | flops 1048576 | bytes 8388608 | tf_op jit(solution)/shard_map/concatenate | solution.py:33
  153.6 9.6 %fusion.16 = f32[1,128,128]{2,1,0:T(8,128)} fusion(f32[1,128,8192]{2,0,1:T(1,128)} %pad_maximum_fusion, f32[64,8192]{1,0:T(8,128)} %concatenate.54, f32[64,8192]{1,0:T(8,128)} %concatenate.53, f32[8192]{0:T(1024)S(1)} %copy-done.3), kind=kOutput, calls=%fused_computation.24 | convolution fusion | flops 1612726272 | bytes 8486912 | tf_op jit(solution)/shard_map/fip,fjp->fij/dot_general | solution.py:35
  163.3 0.7 iota_compare_fusion.4
  163.9 110.4 %all-reduce.2.cloned.1.call-done = f32[1,128,128]{2,1,0:T(8,128)} async-done(((f32[1,128,128]{2,1,0:T(8,128)}), f32[1,128,128]{2,1,0:T(8,128)}) %all-reduce.2.cloned.1.call-update) | async-done | bytes 65552 | tf_op jit(solution)/shard_map/psum | solution.py:102
  274.3 1.5 fusion.34
  275.9 0.7 fusion.19
  277.5 0.2 fusion.29
  277.9 0.2 fusion.11
  278.1 0.2 fusion.38
  278.3 0.2 fusion.37
  278.6 0.2 fusion.10
  278.8 0.2 fusion.40
  279.0 0.2 fusion.39
  279.2 0.2 fusion.9
  279.4 0.2 convolution_bitcast_fusion
  279.6 2.2 fusion.22
  281.8 1.9 fusion.21
  283.7 2.0 fusion.1
  285.8 3.0 %fusion = bf16[1,1,64,8192]{3,2,1,0:T(8,128)(2,1)} fusion(f32[64,8192]{1,0:T(8,128)S(1)} %fusion.21, f32[64,8192]{1,0:T(8,128)S(1)} %copy-done.1, f32[1,128,128]{2,1,0:T(8,128)S(1)} %convolution_bitcast_fusion), kind=kOutput, calls=%fused_computation.1 | convolution fusion | flops 403701760 | bytes 5275648 | tf_op jit(solution)/shard_map/fij,fip->fjp/dot_general | solution.py:82
  289.4 3.0 fusion.5
  (17 shorter events, 0.6 us)
Async XLA Ops:
  7.2 2.2 copy-start
  15.3 10.8 %copy-start.4 = (s32[32]{0:T(128)S(1)}, s32[32]{0:T(128)}, u32[]{:S(2)}) copy-start(s32[32]{0:T(128)} %param.7) | copy-start | bytes 388
  15.3 103.4 %all-to-all-start = ((f32[2,32,2,8192]{3,2,0,1:T(2,128)}), f32[2,32,2,8192]{3,2,0,1:T(2,128)}, u32[]{:S(2)}, u32[]{:S(2)}) async-start(f32[2,32,2,8192]{3,2,0,1:T(2,128)} %copy.10), calls=%async_computation | async-start | bytes 8388608 | tf_op jit(solution)/shard_map/all_to_all | solution.py:100
  26.1 248.3 %all-reduce.2.cloned.1.call-start = ((), (), s32[]{:S(2)}) async-start(), calls=%async_computation.1 | async-start | bytes 131072 | tf_op jit(solution)/shard_map/psum | solution.py:102
  141.3 12.4 %copy-start.3 = (f32[8192]{0:T(1024)S(1)}, f32[8192]{0:T(1024)}, u32[]{:S(2)}) copy-start(f32[8192]{0:T(1024)} %param.5) | copy-start | bytes 98308
  277.3 2.3 copy-start.1
  279.6 2.2 copy-start.2
Sparse Core Ops, SparseCore 0:
  163.4 110.9 all-reduce.1
where the time goes:
time: 301 us; the launch traced here: 300 us
  waiting for transfers between devices  202 us (67%)
  local copies, waits for them, and re-layouts  28.4 us (9%)
  matrix products  21.6 us (7%)
  other arithmetic  19.8 us (7%)
  between operations  17.4 us (6%)
  starting transfers between devices  10.8 us (4%)
    psum x1, waiting for transfers between devices, shards(): summed = lax.psum(partial_value, 'space')  110 us
    all_to_all x1, waiting for transfers between devices, shards(): lax.all_to_all(spectra, 'tm', split_axis=1, concat_axis=2, tiled=True)  92 us
    concatenate x1, other arithmetic, gram_terms(): stacked = jnp.concatenate([spectra_re, spectra_im], axis=1)  12.4 us
    all_to_all x1, starting transfers between devices, shards(): lax.all_to_all(spectra, 'tm', split_axis=1, concat_axis=2, tiled=True)  10.7 us
    dot_general x1, matrix products, gram_terms(): jnp.einsum('fip,fjp->fij', stacked * point_weights[None, None, :], stacke...  9.63 us
    concatenate x2, local copies, waits for them, and re-layouts, gram_terms(): stacked = jnp.concatenate([spectra_re, spectra_im], axis=1)  7.32 us
  transfers between devices with their start and end apart: 2, of which 2 were waited for; matrix products, arithmetic and copies ran while one was open for 0% of the time, Pallas kernels for 0%

commit v1 on v0

--- a/solution.py
+++ b/solution.py
@@ -99,7 +99,7 @@
     spectra = transform_blocks(dft_table, data, freq_count)
     regrouped = lax.all_to_all(spectra, "tm", split_axis=1, concat_axis=2, tiled=True)
     partial_value = gram_terms(regrouped, weights, total_points)
-    summed = lax.psum(partial_value, "space")
+    summed = jnp.sum(lax.all_gather(partial_value, "space"), axis=0)
     kept_counts = lax.dynamic_slice_in_dim(n_keep, lax.axis_index("tm"), 1)
     mode_field, energy = finish_modes(regrouped, summed, kept_counts, block_count)
     return (mode_field, energy)

time: 301 us -> 231 us (0.77)
  waiting for transfers between devices: 202 us -> 45.4 us
  blocking collectives: 0 us -> 102 us
  starting transfers between devices: 10.8 us -> 0.04 us
  local copies, waits for them, and re-layouts: 28.4 us -> 24 us
    psum x1 -> x0, waiting for transfers between devices: 110 us -> none  [shards(): summed = lax.psum(partial_value, 'space')]
    all_to_all x0 -> x1, blocking collectives: none -> 102 us  [shards(): lax.all_to_all(spectra, 'tm', split_axis=1, concat_axis=2, tiled=True)]
    all_to_all x1 -> x0, waiting for transfers between devices: 92 us -> none  [shards(): lax.all_to_all(spectra, 'tm', split_axis=1, concat_axis=2, tiled=True)]
    all_gather x0 -> x1, waiting for transfers between devices: none -> 45.4 us  [shards(): summed = jnp.sum(lax.all_gather(partial_value, 'space'), axis=0)]
    all_to_all x1 -> x0, starting transfers between devices: 10.7 us -> none  [shards(): lax.all_to_all(spectra, 'tm', split_axis=1, concat_axis=2, tiled=True)]
  transfers between devices with their start and end apart: 2 -> 1, of which waited for: 2 -> 1; matrix products, arithmetic and copies ran while one was open for 0% -> 1% of each run, Pallas kernels for 0% -> 0%
where the time goes in v1:
time: 231 us
  blocking collectives  102 us (44%)
  waiting for transfers between devices  45.4 us (20%)
  local copies, waits for them, and re-layouts  24 us (10%)
  matrix products  21.7 us (9%)
  other arithmetic  20.3 us (9%)
  between operations  17.4 us (8%)
    all_to_all x1, blocking collectives, shards(): lax.all_to_all(spectra, 'tm', split_axis=1, concat_axis=2, tiled=True)  102 us
    all_gather x1, waiting for transfers between devices, shards(): summed = jnp.sum(lax.all_gather(partial_value, 'space'), axis=0)  45.4 us
    concatenate x1, other arithmetic, gram_terms(): stacked = jnp.concatenate([spectra_re, spectra_im], axis=1)  12.3 us
    dot_general x1, matrix products, gram_terms(): jnp.einsum('fip,fjp->fij', stacked * point_weights[None, None, :], stacke...  9.63 us
    concatenate x2, local copies, waits for them, and re-layouts, gram_terms(): stacked = jnp.concatenate([spectra_re, spectra_im], axis=1)  7.33 us
    squeeze x1, local copies, waits for them, and re-layouts, gram_terms(): spectra_re = spectra[0]  5.26 us
    squeeze x1, local copies, waits for them, and re-layouts, gram_terms(): spectra_im = spectra[1]  5.23 us
  transfers between devices with their start and end apart: 1, of which 1 were waited for; matrix products, arithmetic and copies ran while one was open for 1% of the time, Pallas kernels for 0%

profile of v1, /device:TPU:1, one launch (start us, length us, event | category | flops | bytes accessed | tf_op | source)
XLA Modules:
  0.0 230.9 jit_solution(18289746690409185046)
XLA Ops:
  7.3 0.7 multiply_reduce_fusion
  8.6 0.8 divide_convert_fusion.1
  9.5 0.7 fusion.33
  10.1 3.2 %copy.11 = f32[2,32,2,8192]{3,2,0,1:T(2,128)S(1)} copy(f32[2,32,2,8192]{3,1,2,0:T(8,128)S(1)} %fusion.33) | data formatting | bytes 8388608 | tf_op jit(solution)/shard_map/rt,btp->rbp/dot_general | solution.py:26
  13.4 102.2 %all_to_all.4 = f32[2,32,2,8192]{3,2,0,1:T(2,128)S(1)} all-to-all(f32[2,32,2,8192]{3,2,0,1:T(2,128)S(1)} %copy.11), channel_id=1, replica_groups=mesh['tm'=32,'space'=16] {'tm'}, dimensions={1} | all-to-all | bytes 8388608 | tf_op jit(solution)/shard_map/all_to_all | solution.py:100
  115.6 2.3 fusion.32
  117.9 5.3 %squeeze.8 = f32[1,64,8192]{2,0,1:T(1,128)} reshape(f32[1,32,2,8192]{3,2,0,1:T(2,128)} %get-tuple-element.6) | data formatting | bytes 4194304 | tf_op jit(solution)/shard_map/squeeze | solution.py:31
  123.1 3.7 %concatenate.53 = f32[64,8192]{1,0:T(8,128)} reshape(f32[1,32,2,8192]{3,2,0,1:T(2,128)} %get-tuple-element.6) | data formatting | bytes 4194304 | tf_op jit(solution)/shard_map/concatenate | solution.py:33
  126.8 5.2 %squeeze.9 = f32[1,64,8192]{2,0,1:T(1,128)} reshape(f32[1,32,2,8192]{3,2,0,1:T(2,128)} %get-tuple-element.7) | data formatting | bytes 4194304 | tf_op jit(solution)/shard_map/squeeze | solution.py:32
  132.1 3.6 %concatenate.54 = f32[64,8192]{1,0:T(8,128)} reshape(f32[1,32,2,8192]{3,2,0,1:T(2,128)} %get-tuple-element.7) | data formatting | bytes 4194304 | tf_op jit(solution)/shard_map/concatenate | solution.py:33
  135.7 12.3 %pad_maximum_fusion = f32[1,128,8192]{2,0,1:T(1,128)} fusion(f32[1,64,8192]{2,0,1:T(1,128)} %squeeze.9, f32[1,64,8192]{2,0,1:T(1,128)} %squeeze.8), kind=kLoop, calls=%fused_computation.8 | loop fusion | flops 1048576 | bytes 8388608 | tf_op jit(solution)/shard_map/concatenate | solution.py:33
  148.1 9.6 %fusion.13 = f32[128,128]{1,0:T(8,128)} fusion(f32[1,128,8192]{2,0,1:T(1,128)} %pad_maximum_fusion, f32[64,8192]{1,0:T(8,128)} %concatenate.54, f32[64,8192]{1,0:T(8,128)} %concatenate.53, f32[8192]{0:T(1024)S(1)} %copy-done.3), kind=kOutput, calls=%fused_computation.23 | convolution fusion | flops 1612726272 | bytes 8486912 | tf_op jit(solution)/shard_map/fip,fjp->fij/dot_general | solution.py:35
  157.7 0.6 dynamic_slice.3
  158.3 0.6 iota_compare_fusion.4
  159.0 45.4 %all-gather.3.cloned.1.call-done = f32[2048,128]{1,0:T(8,128)} async-done(((f32[128,128]{1,0:T(8,128)}), f32[2048,128]{1,0:T(8,128)}) %all-gather.3.cloned.1.call-update) | async-done | bytes 1048592 | tf_op jit(solution)/shard_map/all_gather | solution.py:102
  204.4 1.3 reduce.3
  205.6 0.7 fusion.31
  206.3 0.7 fusion.16
  208.0 0.2 fusion.26
  208.4 0.2 fusion.11
  208.6 0.2 fusion.35
  208.8 0.2 fusion.34
  209.1 0.2 fusion.10
  209.3 0.2 fusion.37
  209.5 0.2 fusion.36
  209.7 0.2 fusion.9
  209.9 0.2 convolution_bitcast_fusion
  210.1 2.2 fusion.19
  212.3 1.9 fusion.18
  214.2 2.0 fusion.1
  216.3 3.0 %fusion = bf16[1,1,64,8192]{3,2,1,0:T(8,128)(2,1)} fusion(f32[64,8192]{1,0:T(8,128)S(1)} %fusion.18, f32[64,8192]{1,0:T(8,128)S(1)} %copy-done.1, f32[1,128,128]{2,1,0:T(8,128)S(1)} %convolution_bitcast_fusion), kind=kOutput, calls=%fused_computation.1 | convolution fusion | flops 403701760 | bytes 5275648 | tf_op jit(solution)/shard_map/fij,fip->fjp/dot_general | solution.py:82
  220.0 3.0 %fusion.5 = bf16[1,2,64,8192]{3,2,1,0:T(8,128)(2,1)} fusion(bf16[1,1,64,8192]{3,2,1,0:T(8,128)(2,1)} %fusion, bf16[1,1,64,8192]{3,2,1,0:T(8,128)(2,1)S(1)} %fusion.1, pred[64]{0:T(512)(128)(4,1)S(1)} %iota_compare_fusion.4), kind=kLoop, calls=%fused_computation.10 | loop fusion | flops 5242880 | bytes 4194368 | tf_op jit(solution)/shard_map/convert_element_type | solution.py:87
  (17 shorter events, 0.6 us)
Async XLA Ops:
  7.2 2.3 copy-start
  7.2 197.2 %all-gather.3.cloned.1.call-start = ((), (), s32[]{:S(2)}) async-start(), calls=%async_computation.1 | async-start | bytes 1114112 | tf_op jit(solution)/shard_map/all_gather | solution.py:102
  135.7 12.3 %copy-start.3 = (f32[8192]{0:T(1024)S(1)}, f32[8192]{0:T(1024)}, u32[]{:S(2)}) copy-start(f32[8192]{0:T(1024)} %param.5) | copy-start | bytes 98308
  148.1 9.7 %copy-start.4 = (s32[32]{0:T(128)S(1)}, s32[32]{0:T(128)}, u32[]{:S(2)}) copy-start(s32[32]{0:T(128)} %param.7) | copy-start | bytes 388
  207.8 2.3 copy-start.1
  210.1 2.2 copy-start.2
Sparse Core Ops, SparseCore 0:
  157.8 46.4 all-gather.2
